TPU v7x, 32 devices: a whole 2x2x4 slice. The times are simulated.
32 devices in a mesh: lon: 8 (over y, x, core), lat: 4 (over z).
Axes of the slice: x: 2, y: 2, z: 4, core: 2. Of those that a mesh axis runs over, the one named last changes fastest.
Arguments:
- obs_rows: bfloat16 [131072, 128], P(('lon', 'lat')), may hold values from -6 to 6
- cell_ids: int32 [131072], P(('lon', 'lat')), may hold values from 0 to 511
- counts: int32 [32, 32], P(('lon', 'lat')), may hold values from 16 to 128, as said below
- w_embed: bfloat16 [128, 256], replicated, may hold values from -0.5 to 0.5
- w_density: bfloat16 [256], replicated, may hold values from -3 to 3
- kernels: bfloat16 [3, 3, 3, 256, 256], replicated, may hold values from -0.125 to 0.125
- cotangent: bfloat16 [64, 256, 256], P('lat', 'lon'), may hold values from -6 to 6
Outputs:
- encoded: bfloat16 [64, 256, 256], P('lat', 'lon')
- grad_kernels: bfloat16 [3, 3, 3, 256, 256], replicated
- grad_embed: bfloat16 [128, 256], replicated
- grad_obs: bfloat16 [131072, 128], P(('lon', 'lat'))
Inputs may be any that keep to these rules, and one draw needn't show every extreme that they name: `counts`: the live rows of each slot are its first ones; in every draw some tile owner receives 128 live rows from every device.
All inputs are finite; a program needn't handle non-finite values.
Results may differ from a plain program's by a relative error of at most 0.011.
Values may be sent and summed in bfloat16 or wider, within the bound.
No kernel may reach another device: no remote copies, remote signals or barrier semaphores. Data moves between devices by JAX's collectives and lax.ppermute only.
A program may use at most 128 MiB of HBM per device.

v0:
```python
import math
import jax
import jax.numpy as jnp
from jax import lax
from jax.sharding import PartitionSpec as P

ID_BASE = 128


def shift_pairs(count, step, periodic):
    pairs = []
    for source in range(count):
        target = source + step
        if 0 <= target < count:
            pairs.append((source, target))
        elif periodic:
            pairs.append((source, target % count))
    return pairs


def widen(block, depth):
    lon_count = lax.axis_size("lon")
    lat_count = lax.axis_size("lat")
    west = lax.ppermute(block[:, -depth:], "lon", shift_pairs(lon_count, 1, True))
    east = lax.ppermute(block[:, :depth], "lon", shift_pairs(lon_count, -1, True))
    block = jnp.concatenate([west, block, east], axis=1)
    north = lax.ppermute(block[-depth:], "lat", shift_pairs(lat_count, 1, False))
    south = lax.ppermute(block[:depth], "lat", shift_pairs(lat_count, -1, False))
    return jnp.concatenate([north, block, south], axis=0)


def lat_mask(rows, margin, height):
    lat_index = lax.axis_index("lat")
    lat_count = lax.axis_size("lat")
    global_row = lat_index * height - margin + jnp.arange(rows, dtype=jnp.int32)
    return ((global_row >= 0) & (global_row < lat_count * height))[:, None, None]


def crop(field, margin):
    if margin == 0:
        return field
    return field[margin:-margin, margin:-margin]


def conv_valid(padded, kernel):
    return lax.conv_general_dilated(
        padded[None],
        kernel,
        (1, 1),
        "VALID",
        dimension_numbers=("NHWC", "HWIO", "NHWC"),
        preferred_element_type=jnp.float32,
    )[0]


def reduce_replicated(parts):
    flat = jnp.concatenate([part.reshape(-1) for part in parts])
    summed = lax.psum_scatter(flat, ("lon", "lat"), scatter_dimension=0, tiled=True)
    return summed


def on_device(obs_rows, cell_ids, counts, w_embed, w_density, kernels, cotangent):
    lon_count = lax.axis_size("lon")
    lat_count = lax.axis_size("lat")
    devices = lon_count * lat_count
    height, tile_width, channels = cotangent.shape
    cell_count = height * tile_width
    slot_rows = obs_rows.shape[0] // devices
    feat_count = obs_rows.shape[1]
    layer_count = kernels.shape[0]
    margin = 2 * layer_count
    cot_wide = widen(cotangent, layer_count)
    live_mask = jnp.arange(slot_rows, dtype=jnp.int32)[None, :] < counts[0][:, None]
    slot_ids = cell_ids.reshape(devices, slot_rows)
    id_high = jnp.where(live_mask, slot_ids // ID_BASE, -1)
    id_low = jnp.where(live_mask, slot_ids % ID_BASE, -1)
    code = jnp.concatenate([id_high, id_low], axis=1).astype(jnp.bfloat16)
    code_rows = -(-2 * slot_rows // feat_count)
    code_pad = -(-code_rows // 16) * 16
    code = jnp.pad(code, ((0, 0), (0, code_rows * feat_count - 2 * slot_rows)))
    code = code.reshape(devices, code_rows, feat_count)
    code = jnp.pad(code, ((0, 0), (0, code_pad - code_rows), (0, 0)))
    packed = jnp.concatenate([obs_rows.reshape(devices, slot_rows, feat_count), code], axis=1)
    got = lax.all_to_all(packed, ("lon", "lat"), split_axis=0, concat_axis=0, tiled=True)
    got_rows = got[:, :slot_rows].reshape(devices * slot_rows, feat_count)
    got_code = got[:, slot_rows : slot_rows + code_rows].reshape(devices, code_rows * feat_count)
    got_code = got_code.astype(jnp.int32)
    got_ids = (got_code[:, :slot_rows] * ID_BASE + got_code[:, slot_rows : 2 * slot_rows]).reshape(
        -1
    )
    cell_iota = jnp.arange(cell_count, dtype=jnp.int32)
    onehot = (got_ids[:, None] == cell_iota[None, :]).astype(jnp.bfloat16)
    cell_sums = lax.dot_general(
        onehot, got_rows, (((0,), (0,)), ((), ())), preferred_element_type=jnp.float32
    )
    density = jnp.sum(onehot.astype(jnp.float32), axis=0)
    inv_root = lax.rsqrt(density + 1.0)
    features = (cell_sums * inv_root[:, None]).astype(jnp.bfloat16)
    start_act = (
        jnp.dot(features, w_embed, preferred_element_type=jnp.float32)
        + jnp.log1p(density)[:, None] * w_density.astype(jnp.float32)[None, :]
    )
    activation = start_act.astype(jnp.bfloat16).reshape(height, tile_width, channels)
    act = widen(activation, margin)
    stored_acts = [act]
    stored_pre = []
    for layer_index in range(layer_count):
        out_margin = margin - layer_index - 1
        preact = conv_valid(act, kernels[layer_index])
        act = (crop(act, 1).astype(jnp.float32) + jax.nn.silu(preact)).astype(jnp.bfloat16)
        act = jnp.where(lat_mask(act.shape[0], out_margin, height), act, jnp.zeros_like(act))
        stored_pre.append(preact)
        stored_acts.append(act)
    encoded = crop(act, margin - layer_count)
    grad_scale = 1.0 / math.sqrt(cell_count * devices)
    back = cot_wide
    reduced = [None] * layer_count
    for layer_index in reversed(range(layer_count)):
        back_margin = layer_index + 1
        preact = crop(stored_pre[layer_index], margin - layer_index - 1 - back_margin)
        sigmoid_v = jax.nn.sigmoid(preact)
        slope = (
            back.astype(jnp.float32) * (sigmoid_v * (1.0 + preact * (1.0 - sigmoid_v)))
        ).astype(jnp.bfloat16)
        slope = jnp.where(
            lat_mask(slope.shape[0], back_margin, height), slope, jnp.zeros_like(slope)
        )
        slope_flat = crop(slope, back_margin).reshape(cell_count, channels)
        act_in = crop(stored_acts[layer_index], margin - layer_index - 1)
        tap_rows = []
        for row_off in range(3):
            tap_cols = []
            for col_off in range(3):
                window = act_in[row_off : row_off + height, col_off : col_off + tile_width].reshape(
                    cell_count, channels
                )
                tap_cols.append(
                    lax.dot_general(
                        window,
                        slope_flat,
                        (((0,), (0,)), ((), ())),
                        preferred_element_type=jnp.float32,
                    )
                )
            tap_rows.append(jnp.stack(tap_cols))
        tap_grad = jnp.stack(tap_rows)
        flipped = jnp.transpose(kernels[layer_index][::-1, ::-1], (0, 1, 3, 2))
        spread = conv_valid(slope, flipped)
        back = lax.optimization_barrier(
            (crop(back, 1).astype(jnp.float32) + spread).astype(jnp.bfloat16)
        )
        if layer_index > 0:
            reduced[layer_index] = reduce_replicated([tap_grad])
        else:
            last_grad = tap_grad
    back_flat = back.reshape(cell_count, channels)
    embed_grad = lax.dot_general(
        features, back_flat, (((0,), (0,)), ((), ())), preferred_element_type=jnp.float32
    )
    reduced[0] = reduce_replicated([last_grad, embed_grad])
    cell_grad = (
        lax.dot_general(
            back_flat, w_embed, (((1,), (1,)), ((), ())), preferred_element_type=jnp.float32
        )
        * inv_root[:, None]
    ).astype(jnp.bfloat16)
    picked = jnp.dot(onehot, cell_grad, preferred_element_type=jnp.float32).astype(jnp.bfloat16)
    grad_obs = lax.all_to_all(picked, ("lon", "lat"), split_axis=0, concat_axis=0, tiled=True)
    tap_size = kernels[0].size
    gathered = [
        lax.all_gather((part * grad_scale).astype(jnp.bfloat16), ("lon", "lat"), axis=0, tiled=True)
        for part in reduced
    ]
    kernel_out = jnp.stack(
        [gathered[0][:tap_size]] + [gathered[index] for index in range(1, layer_count)]
    ).reshape(kernels.shape)
    embed_out = gathered[0][tap_size:].reshape(w_embed.shape)
    return (encoded, kernel_out, embed_out, grad_obs)


def solution(mesh):
    placed = (
        P(("lon", "lat"), None),
        P(("lon", "lat")),
        P(("lon", "lat"), None),
        P(),
        P(),
        P(),
        P("lat", "lon", None),
    )
    return jax.shard_map(
        on_device,
        mesh=mesh,
        in_specs=placed,
        out_specs=(P("lat", "lon", None), P(), P(), P(("lon", "lat"), None)),
        check_vma=False,
    )
```

profile of v0, /device:TPU:0, one launch (start us, length us, event | category | flops | bytes accessed | tf_op | source)
XLA Modules:
  0.0 475.4 jit_solution(3114485129641464012)
XLA Ops:
  7.2 0.9 fusion.119
  8.0 0.8 fusion.120
  8.9 2.3 pad_maximum_fusion.5
  11.2 7.3 %all-to-all-start = ((bf16[32,144,128]{2,1,0:T(8,128)(2,1)}), bf16[32,144,128]{2,1,0:T(8,128)(2,1)S(1)}, u32[]{:S(2)}, u32[]{:S(2)}) async-start(bf16[32,144,128]{2,1,0:T(8,128)(2,1)} %pad_maximum_fusion.5), calls=%async_computation | async-start | bytes 2359296 | tf_op jit(solution)/shard_map/all_to_all | solution.py:84
  18.6 2.5 collective-permute-start.5
  21.1 0.5 compare_and_fusion.2
  21.7 4.4 collective-permute-done.5
  26.1 2.8 collective-permute-done.4
  28.9 0.9 fusion.160
  29.8 16.5 %all-to-all-done = bf16[32,144,128]{2,1,0:T(8,128)(2,1)S(1)} async-done(((bf16[32,144,128]{2,1,0:T(8,128)(2,1)}), bf16[32,144,128]{2,1,0:T(8,128)(2,1)S(1)}, u32[]{:S(2)}, u32[]{:S(2)}) %all-to-all-start) | async-done | bytes 1179680 | tf_op jit(solution)/shard_map/all_to_all | solution.py:84
  46.3 1.0 convert_reduce_fusion
  47.5 3.0 fusion.19
  50.7 2.7 collective-permute-start.1
  53.4 1.3 collective-permute-start.7
  54.7 4.6 collective-permute-start.6
  59.5 1.3 collective-permute-start.3
  60.8 4.6 collective-permute-start.2
  65.3 0.6 slice.307
  65.9 0.9 pad_maximum_fusion.8
  67.2 1.2 collective-permute-done.2
  69.1 0.4 copy.76
  69.7 2.9 convolution_select_fusion
  72.6 0.5 copy.77
  73.3 1.1 pad_maximum_fusion.6
  74.4 0.5 broadcast_select_fusion
  75.0 0.9 pad.7
  75.9 1.8 reshape.308
  77.9 2.8 convolution_select_fusion.1
  80.7 0.7 copy.80
  81.5 0.6 broadcast_select_fusion.1
  82.5 1.0 copy-done.18
  83.5 1.3 add_multiply_fusion
  85.2 0.4 broadcast_subtract_fusion
  85.8 0.7 copy-done.1
  86.6 1.2 fusion.84
  91.0 0.9 copy-done.5
  93.0 1.2 convolution_select_fusion.3
  94.8 0.4 broadcast_select_fusion.2
  95.5 0.5 convolution_bitcast_fusion.10
  98.7 0.4 copy-done.21
  99.1 1.1 convolution_select_fusion.4
  104.2 2.6 copy.118
  107.1 2.7 copy.117
  110.1 0.4 copy-done.20
  110.5 1.0 convolution_select_fusion.5
  112.1 0.5 copy-done.9
  114.1 1.2 copy.115
  115.4 1.6 pad_maximum_fusion.1
  117.0 166.5 %all-reduce.7.cloned.1.call-done = (f32[589824]{0:T(1024)}, f32[589824]{0:T(1024)}, f32[622592]{0:T(1024)}) async-done(((f32[589824]{0:T(1024)}, f32[589824]{0:T(1024)}, f32[622592]{0:T(1024)}), (f32[589824]{0:T(1024)}, f32[589824]{0:T(1024)}, f32[622592]{0:T(1024)})) %all-reduce.7.cloned.1.call-update) | async-done | bytes 7208976
  283.5 1.5 fusion.117
  285.1 1.5 fusion.118
  286.7 1.5 fusion.116
  288.2 1.7 fusion.3
  290.0 30.8 %all_to_all.17 = bf16[32,128,128]{2,1,0:T(8,128)(2,1)S(1)} all-to-all(bf16[32,128,128]{2,1,0:T(8,128)(2,1)S(1)} %bitcast.273), channel_id=1, replica_groups=mesh['lon'=8,'lat'=4] {'lon','lat'}, dimensions={0} | all-to-all | bytes 2097152 | tf_op jit(solution)/shard_map/all_to_all | solution.py:168
  320.8 24.1 %all-gather.8.cloned.1.call-done = bf16[589824]{0:T(1024)(128)(2,1)} async-done(((bf16[18432]{0:T(1024)(128)(2,1)}), bf16[589824]{0:T(1024)(128)(2,1)}) %all-gather.8.cloned.1.call-update) | async-done | bytes 1179664 | tf_op jit(solution)/shard_map/all_gather | solution.py:171
  344.9 2.2 stack.206
  347.1 54.6 %all-gather.6.cloned.1.call-done = bf16[589824]{0:T(1024)(128)(2,1)} async-done(((bf16[18432]{0:T(1024)(128)(2,1)}), bf16[589824]{0:T(1024)(128)(2,1)}) %all-gather.6.cloned.1.call-update) | async-done | bytes 1179664 | tf_op jit(solution)/shard_map/all_gather | solution.py:171
  401.7 2.2 stack.189
  403.9 54.7 %all-gather.4.cloned.1.call-done = bf16[622592]{0:T(1024)(128)(2,1)} async-done(((bf16[19456]{0:T(1024)(128)(2,1)}), bf16[622592]{0:T(1024)(128)(2,1)}) %all-gather.4.cloned.1.call-update) | async-done | bytes 1245200 | tf_op jit(solution)/shard_map/all_gather | solution.py:171
  458.6 2.4 slice.329
  461.0 3.0 stack.172
  464.0 0.7 slice.275
  464.7 3.0 pad_maximum_fusion
  467.7 1.0 copy.155
  (159 shorter events, 17.8 us)
Async XLA Ops:
  7.2 43.3 %copy-start = (bf16[128,256]{1,0:T(8,128)(2,1)S(1)}, bf16[128,256]{1,0:T(8,128)(2,1)}, u32[]{:S(2)}) copy-start(bf16[128,256]{1,0:T(8,128)(2,1)} %param.10) | copy-start | bytes 196612
  11.2 7.4 %copy-start.4 = (bf16[16,32,256]{2,1,0:T(8,128)(2,1)S(1)}, bf16[16,32,256]{2,1,0:T(8,128)(2,1)}, u32[]{:S(2)}) copy-start(bf16[16,32,256]{2,1,0:T(8,128)(2,1)} %param.13) | copy-start | bytes 786436
  11.2 10.4 %copy-start.19 = (bf16[256]{0:T(256)(128)(2,1)S(1)}, bf16[256]{0:T(256)(128)(2,1)}, u32[]{:S(2)}) copy-start(bf16[256]{0:T(256)(128)(2,1)} %param.11) | copy-start | bytes 1540
  11.2 35.1 %all-to-all-start = ((bf16[32,144,128]{2,1,0:T(8,128)(2,1)}), bf16[32,144,128]{2,1,0:T(8,128)(2,1)S(1)}, u32[]{:S(2)}, u32[]{:S(2)}) async-start(bf16[32,144,128]{2,1,0:T(8,128)(2,1)} %pad_maximum_fusion.5), calls=%async_computation | async-start | bytes 2359296 | tf_op jit(solution)/shard_map/all_to_all | solution.py:84
  18.5 265.0 %all-reduce.7.cloned.1.call-start = ((), (), s32[]{:S(2)}) async-start(), calls=%async_computation.5 | async-start | bytes 14417920
  18.6 7.5 %collective-permute-start.5 = (bf16[16,3,256]{2,1,0:T(4,128)(2,1)S(1)}, bf16[16,3,256]{2,1,0:T(4,128)(2,1)S(1)}, u32[]{:S(2)}, u32[]{:S(2)}) collective-permute-start(bf16[16,3,256]{2,1,0:T(4,128)(2,1)S(1)} %get-tuple-element.22), channel_id=1, source_target_pairs={{0,28},{4,0},{8,4},{12,8},{16,12},{20,16},{24,20},{28,24},{1,29},{... | collective-permute-start | bytes 73736 | tf_op jit(solution)/shard_map/ppermute | solution.py:25
  21.1 7.8 %collective-permute-start.4 = (bf16[16,3,256]{2,1,0:T(4,128)(2,1)S(1)}, bf16[16,3,256]{2,1,0:T(4,128)(2,1)S(1)}, u32[]{:S(2)}, u32[]{:S(2)}) collective-permute-start(bf16[16,3,256]{2,1,0:T(4,128)(2,1)S(1)} %get-tuple-element.21), channel_id=1, source_target_pairs={{0,4},{4,8},{8,12},{12,16},{16,20},{20,24},{24,28},{28,0},{1,5},{5... | collective-permute-start | bytes 73736 | tf_op jit(solution)/shard_map/ppermute | solution.py:24
  21.6 43.7 %copy-start.14 = (pred[22]{0:T(512)(128)(4,1)}, pred[22]{0:T(512)(128)(4,1)S(1)}, u32[]{:S(2)}) copy-start(pred[22]{0:T(512)(128)(4,1)S(1)} %compare_and_fusion.4) | copy-start | bytes 70
  50.4 9.0 %copy-start.8 = (bf16[512,128]{1,0:T(8,128)(2,1)}, bf16[512,128]{1,0:T(8,128)(2,1)S(1)}, u32[]{:S(2)}) copy-start(bf16[512,128]{1,0:T(8,128)(2,1)S(1)} %fusion.19) | copy-start | bytes 393220
  50.7 8.6 %collective-permute-start.1 = (bf16[16,6,256]{2,1,0:T(8,128)(2,1)S(1)}, bf16[16,6,256]{2,1,0:T(8,128)(2,1)S(1)}, u32[]{:S(2)}, u32[]{:S(2)}) collective-permute-start(bf16[16,6,256]{2,1,0:T(8,128)(2,1)S(1)} %get-tuple-element.24), channel_id=1, source_target_pairs={{0,28},{4,0},{8,4},{12,8},{16,12},{20,16},{24,20},{28,24},{1,29},{... | collective-permute-start | bytes 147464 | tf_op jit(solution)/shard_map/ppermute | solution.py:25
  53.4 5.9 %collective-permute-start = (bf16[16,6,256]{2,1,0:T(8,128)(2,1)S(1)}, bf16[16,6,256]{2,1,0:T(8,128)(2,1)S(1)}, u32[]{:S(2)}, u32[]{:S(2)}) collective-permute-start(bf16[16,6,256]{2,1,0:T(8,128)(2,1)S(1)} %get-tuple-element.23), channel_id=1, source_target_pairs={{0,4},{4,8},{8,12},{12,16},{16,20},{20,24},{24,28},{28,0},{1,5},{5... | collective-permute-start | bytes 147464 | tf_op jit(solution)/shard_map/ppermute | solution.py:24
  53.4 12.5 %collective-permute-start.7 = (bf16[3,38,256]{2,1,0:T(8,128)(2,1)S(1)}, bf16[3,38,256]{2,1,0:T(8,128)(2,1)S(1)}, u32[]{:S(2)}, u32[]{:S(2)}) collective-permute-start(bf16[3,38,256]{2,1,0:T(8,128)(2,1)S(1)} %get-tuple-element.20), channel_id=1, source_target_pairs={{1,0},{2,1},{3,2},{5,4},{6,5},{7,6},{9,8},{10,9},{11,10},{13,12},{... | collective-permute-start | bytes 175112 | tf_op jit(solution)/shard_map/ppermute | solution.py:28
  54.7 11.2 %collective-permute-start.6 = (bf16[3,38,256]{2,1,0:T(8,128)(2,1)S(1)}, bf16[3,38,256]{2,1,0:T(8,128)(2,1)S(1)}, u32[]{:S(2)}, u32[]{:S(2)}) collective-permute-start(bf16[3,38,256]{2,1,0:T(8,128)(2,1)S(1)} %get-tuple-element.19), channel_id=1, source_target_pairs={{0,1},{1,2},{2,3},{4,5},{5,6},{6,7},{8,9},{9,10},{10,11},{12,13},{... | collective-permute-start | bytes 175112 | tf_op jit(solution)/shard_map/ppermute | solution.py:27
  59.3 9.2 %copy-start.6 = (bf16[16,6,256]{2,1,0:T(8,128)(2,1)}, bf16[16,6,256]{2,1,0:T(8,128)(2,1)S(1)}, u32[]{:S(2)}) copy-start(bf16[16,6,256]{2,1,0:T(8,128)(2,1)S(1)} %collective-permute-done) | copy-start | bytes 147460
  59.5 7.7 %collective-permute-start.3 = (bf16[6,44,256]{2,1,0:T(8,128)(2,1)S(1)}, bf16[6,44,256]{2,1,0:T(8,128)(2,1)S(1)}, u32[]{:S(2)}, u32[]{:S(2)}) collective-permute-start(bf16[6,44,256]{2,1,0:T(8,128)(2,1)S(1)} %get-tuple-element.16), channel_id=1, source_target_pairs={{1,0},{2,1},{3,2},{5,4},{6,5},{7,6},{9,8},{10,9},{11,10},{13,12},{... | collective-permute-start | bytes 405512 | tf_op jit(solution)/shard_map/ppermute | solution.py:28
  60.8 7.6 %collective-permute-start.2 = (bf16[6,44,256]{2,1,0:T(8,128)(2,1)S(1)}, bf16[6,44,256]{2,1,0:T(8,128)(2,1)S(1)}, u32[]{:S(2)}, u32[]{:S(2)}) collective-permute-start(bf16[6,44,256]{2,1,0:T(8,128)(2,1)S(1)} %get-tuple-element.15), channel_id=1, source_target_pairs={{0,1},{1,2},{2,3},{4,5},{5,6},{6,7},{8,9},{9,10},{10,11},{12,13},{... | collective-permute-start | bytes 405512 | tf_op jit(solution)/shard_map/ppermute | solution.py:27
  65.9 2.9 copy-start.10
  65.9 2.9 copy-start.12
  68.4 0.7 copy-start.2
  69.0 0.7 copy-start.25
  73.3 1.1 copy-start.16
  75.9 2.0 copy-start.24
  81.5 2.0 copy-start.18
  82.1 1.3 copy-start.23
  85.6 1.0 copy-start.1
  85.6 1.0 copy-start.17
  90.9 1.0 copy-start.5
  90.9 1.0 copy-start.11
  91.0 1.0 copy-start.13
  91.0 1.0 copy-start.15
  92.3 0.7 copy-start.22
  98.4 0.7 copy-start.21
  100.5 0.9 copy-start.3
  100.5 0.9 copy-start.7
  109.8 0.7 copy-start.20
  111.7 0.9 copy-start.9
  117.0 227.9 %all-gather.8.cloned.1.call-start = ((), (), s32[]{:S(2)}) async-start(), calls=%async_computation.4 | async-start | bytes 1216512 | tf_op jit(solution)/shard_map/all_gather | solution.py:171
  285.1 116.6 %all-gather.6.cloned.1.call-start = ((), (), s32[]{:S(2)}) async-start(), calls=%async_computation.3 | async-start | bytes 1216512 | tf_op jit(solution)/shard_map/all_gather | solution.py:171
  286.7 172.0 %all-gather.4.cloned.1.call-start = ((), (), s32[]{:S(2)}) async-start(), calls=%async_computation.2 | async-start | bytes 1284096 | tf_op jit(solution)/shard_map/all_gather | solution.py:171
  461.0 3.0 slice-start
Sparse Core Ops, SparseCore 0:
  117.1 166.3 all-reduce.6
  287.3 57.5 all-gather.7
  348.6 53.0 all-gather.5
  405.5 53.1 all-gather.3
where the time goes:
time: 484 us; the launch traced here: 475 us
  waiting for transfers between devices  325 us (67%)
  local copies, waits for them, and re-layouts  31.8 us (7%)
  blocking collectives  30.8 us (6%)
  other arithmetic  24.4 us (5%)
  starting transfers between devices  24.4 us (5%)
  matrix products  23.7 us (5%)
  between operations  15.1 us (3%)
    unnamed x5, waiting for transfers between devices  167 us
    all_gather x3, waiting for transfers between devices, on_device(): lax.all_gather((part * grad_scale).astype(jnp.bfloat16), ('lon', 'lat'),...  133 us
    all_to_all x1, blocking collectives, on_device(): lax.all_to_all(picked, ('lon', 'lat'), split_axis=0, concat_axis=0, tiled...  30.8 us
    all_to_all x1, waiting for transfers between devices, on_device(): lax.all_to_all(packed, ('lon', 'lat'), split_axis=0, concat_axis=0, tiled...  16.5 us
    unnamed x63, local copies, waits for them, and re-layouts  13.4 us
    conv_general_dilated x6, matrix products, conv_valid(): lax.conv_general_dilated(padded[None], kernel, (1, 1), 'VALID', dimension...  10.2 us
  transfers between devices with their start and end apart: 13, of which 9 were waited for; matrix products, arithmetic and copies ran while one was open for 3% of the time, Pallas kernels for 0%

commit v1 on v0

--- a/solution.py
+++ b/solution.py
@@ -5,6 +5,18 @@
 from jax.sharding import PartitionSpec as P
 
 ID_BASE = 128
+
+
+def collect(shard, axis, dim):
+    ways, here, turn = (lax.axis_size(axis), lax.axis_index(axis), shard.shape[dim])
+    line, have = (shard, 1)
+    while have < ways:
+        line = jnp.concatenate(
+            [line, lax.ppermute(line, axis, [(d, (d - have) % ways) for d in range(ways)])],
+            axis=dim,
+        )
+        have = 2 * have
+    return jnp.roll(line, here * turn, axis=dim)
 
 
 def shift_pairs(count, step, periodic):
@@ -168,8 +180,7 @@
     grad_obs = lax.all_to_all(picked, ("lon", "lat"), split_axis=0, concat_axis=0, tiled=True)
     tap_size = kernels[0].size
     gathered = [
-        lax.all_gather((part * grad_scale).astype(jnp.bfloat16), ("lon", "lat"), axis=0, tiled=True)
-        for part in reduced
+        collect((part * grad_scale).astype(jnp.bfloat16), ("lon", "lat"), 0) for part in reduced
     ]
     kernel_out = jnp.stack(
         [gathered[0][:tap_size]] + [gathered[index] for index in range(1, layer_count)]

time: 484 us -> 423 us (0.87)
  the two profiles are of different devices: /device:TPU:0 before, /device:TPU:27 now
where the time goes in v1:
time: 423 us; the launch traced here: 415 us
  waiting for transfers between devices  263 us (62%)
  local copies, waits for them, and re-layouts  42.3 us (10%)
  starting transfers between devices  36.1 us (9%)
  other arithmetic  33.1 us (8%)
  matrix products  24.9 us (6%)
  between operations  15.6 us (4%)
    unnamed x2, waiting for transfers between devices  145 us
    ppermute x15, waiting for transfers between devices, collect(): lax.ppermute(line, axis, [(d, (d - have) % ways) for d in range(ways)])  57.7 us
    all_to_all x1, waiting for transfers between devices, on_device(): lax.all_to_all(picked, ('lon', 'lat'), split_axis=0, concat_axis=0, tiled...  34.2 us
    unnamed x93, local copies, waits for them, and re-layouts  21.4 us
    all_to_all x1, waiting for transfers between devices, on_device(): lax.all_to_all(packed, ('lon', 'lat'), split_axis=0, concat_axis=0, tiled...  14.3 us
    conv_general_dilated x6, matrix products, conv_valid(): lax.conv_general_dilated(padded[None], kernel, (1, 1), 'VALID', dimension...  10.2 us
    concatenate x2, other arithmetic, collect(): return jnp.roll(line, here * turn, axis=dim)  10 us
    ppermute x15, starting transfers between devices, collect(): lax.ppermute(line, axis, [(d, (d - have) % ways) for d in range(ways)])  9.13 us
  transfers between devices with their start and end apart: 26, of which 20 were waited for; matrix products, arithmetic and copies ran while one was open for 6% of the time, Pallas kernels for 0%

profile of v1, /device:TPU:27, one launch (start us, length us, event | category | flops | bytes accessed | tf_op | source)
XLA Modules:
  0.0 415.0 jit_solution(7402610779682844918)
XLA Ops:
  8.9 2.3 pad_maximum_fusion.5
  11.2 6.2 %all-to-all-start = ((bf16[32,144,128]{2,1,0:T(8,128)(2,1)}), bf16[32,144,128]{2,1,0:T(8,128)(2,1)S(1)}, u32[]{:S(2)}, u32[]{:S(2)}) async-start(bf16[32,144,128]{2,1,0:T(8,128)(2,1)} %pad_maximum_fusion.5), calls=%async_computation | async-start | bytes 2359296 | tf_op jit(solution)/shard_map/all_to_all | solution.py:96
  17.9 2.3 collective-permute-start.4
  20.7 7.6 %collective-permute-done.5 = bf16[16,3,256]{2,1,0:T(4,128)(2,1)S(1)} collective-permute-done((bf16[16,3,256]{2,1,0:T(4,128)(2,1)S(1)}, bf16[16,3,256]{2,1,0:T(4,128)(2,1)S(1)}, u32[]{:S(2)}, u32[]{:S(2)}) %collective-permute-start.5) | collective-permute-done | bytes 24608 | tf_op jit(solution)/shard_map/ppermute | solution.py:37
  29.3 14.3 %all-to-all-done = bf16[32,144,128]{2,1,0:T(8,128)(2,1)S(1)} async-done(((bf16[32,144,128]{2,1,0:T(8,128)(2,1)}), bf16[32,144,128]{2,1,0:T(8,128)(2,1)S(1)}, u32[]{:S(2)}, u32[]{:S(2)}) %all-to-all-start) | async-done | bytes 1179680 | tf_op jit(solution)/shard_map/all_to_all | solution.py:96
  43.6 1.0 convert_reduce_fusion
  44.8 3.0 fusion.21
  48.0 1.6 collective-permute-start.1
  49.6 1.1 collective-permute-start
  50.7 3.4 collective-permute-start.7
  54.1 1.3 collective-permute-start.6
  55.6 4.0 collective-permute-start.3
  59.6 1.3 collective-permute-start.2
  61.5 0.9 pad_maximum_fusion.8
  62.4 4.0 collective-permute-done.2
  67.8 2.9 convolution_select_fusion
  71.4 1.1 pad_maximum_fusion.6
  74.0 1.5 reshape.308
  75.7 2.8 convolution_select_fusion.1
  80.3 1.0 copy-done.24
  81.3 1.3 add_multiply_fusion
  84.4 1.2 fusion.86
  90.8 1.2 convolution_select_fusion.3
  97.2 1.1 convolution_select_fusion.4
  102.2 2.6 copy.118
  105.2 2.6 copy.117
  108.5 1.0 convolution_select_fusion.5
  112.1 1.2 copy.115
  113.3 1.6 pad_maximum_fusion.1
  115.0 2.7 fusion.3
  117.7 5.4 %all-to-all-start.1 = ((bf16[32,128,128]{2,1,0:T(8,128)(2,1)}), bf16[32,128,128]{2,1,0:T(8,128)(2,1)S(1)}, u32[]{:S(2)}, u32[]{:S(2)}) async-start(bf16[32,128,128]{2,1,0:T(8,128)(2,1)} %bitcast.105), calls=%async_computation.1 | async-start | bytes 2097152 | tf_op jit(solution)/shard_map/all_to_all | solution.py:180
  123.1 34.2 %all-to-all-done.1 = bf16[32,128,128]{2,1,0:T(8,128)(2,1)S(1)} async-done(((bf16[32,128,128]{2,1,0:T(8,128)(2,1)}), bf16[32,128,128]{2,1,0:T(8,128)(2,1)S(1)}, u32[]{:S(2)}, u32[]{:S(2)}) %all-to-all-start.1) | async-done | bytes 1048608 | tf_op jit(solution)/shard_map/all_to_all | solution.py:180
  157.3 145.0 %all-reduce.7.cloned.1.call-done = (f32[589824]{0:T(1024)}, f32[589824]{0:T(1024)}, f32[622592]{0:T(1024)}) async-done(((f32[589824]{0:T(1024)}, f32[589824]{0:T(1024)}, f32[622592]{0:T(1024)}), (f32[589824]{0:T(1024)}, f32[589824]{0:T(1024)}, f32[622592]{0:T(1024)})) %all-reduce.7.cloned.1.call-update) | async-done | bytes 7208976
  303.2 1.0 collective-permute-start.18
  305.4 1.5 constant_dynamic-update-slice_fusion
  307.8 2.4 collective-permute-done.18
  310.2 1.5 collective-permute-start.19
  312.1 1.9 collective-permute-done.8
  314.9 7.3 %collective-permute-done.19 = bf16[36864]{0:T(1024)(128)(2,1)S(1)} collective-permute-done((bf16[36864]{0:T(1024)(128)(2,1)S(1)}, bf16[36864]{0:T(1024)(128)(2,1)S(1)}, u32[]{:S(2)}, u32[]{:S(2)}) %collective-permute-start.19) | collective-permute-done | bytes 73760 | tf_op jit(solution)/shard_map/ppermute | solution.py:15
  322.2 1.5 collective-permute-done.14
  325.4 2.2 collective-permute-done.20
  327.7 1.5 collective-permute-done.15
  329.3 0.9 collective-permute-start.16
  330.9 0.9 collective-permute-start.11
  332.6 5.1 %collective-permute-done.21 = bf16[147456]{0:T(1024)(128)(2,1)S(1)} collective-permute-done((bf16[147456]{0:T(1024)(128)(2,1)S(1)}, bf16[147456]{0:T(1024)(128)(2,1)S(1)}, u32[]{:S(2)}, u32[]{:S(2)}) %collective-permute-start.21) | collective-permute-done | bytes 294944 | tf_op jit(solution)/shard_map/ppermute | solution.py:15
  337.8 1.3 collective-permute-start.22
  339.0 5.0 %collective-permute-done.16 = bf16[147456]{0:T(1024)(128)(2,1)S(1)} collective-permute-done((bf16[147456]{0:T(1024)(128)(2,1)S(1)}, bf16[147456]{0:T(1024)(128)(2,1)S(1)}, u32[]{:S(2)}, u32[]{:S(2)}) %collective-permute-start.16) | collective-permute-done | bytes 294944 | tf_op jit(solution)/shard_map/ppermute | solution.py:15
  344.1 1.3 collective-permute-start.17
  345.4 4.9 %collective-permute-done.11 = bf16[155648]{0:T(1024)(128)(2,1)S(1)} collective-permute-done((bf16[155648]{0:T(1024)(128)(2,1)S(1)}, bf16[155648]{0:T(1024)(128)(2,1)S(1)}, u32[]{:S(2)}, u32[]{:S(2)}) %collective-permute-start.11) | collective-permute-done | bytes 311328 | tf_op jit(solution)/shard_map/ppermute | solution.py:15
  350.3 0.9 constant_dynamic-update-slice_fusion.22
  351.3 1.2 collective-permute-start.12
  352.5 10.6 %collective-permute-done.22 = bf16[294912]{0:T(1024)(128)(2,1)S(1)} collective-permute-done((bf16[294912]{0:T(1024)(128)(2,1)S(1)}, bf16[294912]{0:T(1024)(128)(2,1)S(1)}, u32[]{:S(2)}, u32[]{:S(2)}) %collective-permute-start.22) | collective-permute-done | bytes 589856 | tf_op jit(solution)/shard_map/ppermute | solution.py:15
  363.2 4.5 %fusion.11 = bf16[589824]{0:T(1024)(128)(2,1)S(1)} fusion(s32[]{:T(128)S(6)} %select_n.100, bf16[589824]{0:T(1024)(128)(2,1)S(1)} %constant_dynamic-update-slice_fusion.31), kind=kLoop, calls=%fused_computation.35 | loop fusion | flops 2359296 | bytes 2359300 | tf_op jit(solution)/shard_map/jit(_roll_dynamic)/concatenate | solution.py:19
  367.6 8.1 %collective-permute-done.17 = bf16[294912]{0:T(1024)(128)(2,1)S(1)} collective-permute-done((bf16[294912]{0:T(1024)(128)(2,1)S(1)}, bf16[294912]{0:T(1024)(128)(2,1)S(1)}, u32[]{:S(2)}, u32[]{:S(2)}) %collective-permute-start.17) | collective-permute-done | bytes 589856 | tf_op jit(solution)/shard_map/ppermute | solution.py:15
  375.8 5.5 %fusion.12 = bf16[589824]{0:T(1024)(128)(2,1)} fusion(s32[]{:T(128)S(6)} %select_n.100, bf16[589824]{0:T(1024)(128)(2,1)S(1)} %constant_dynamic-update-slice_fusion.30), kind=kLoop, calls=%fused_computation.36 | loop fusion | flops 2359296 | bytes 2359300 | tf_op jit(solution)/shard_map/jit(_roll_dynamic)/concatenate | solution.py:19
  381.7 2.2 stack.189
  384.0 5.2 %collective-permute-done.12 = bf16[311296]{0:T(1024)(128)(2,1)} collective-permute-done((bf16[311296]{0:T(1024)(128)(2,1)}, bf16[311296]{0:T(1024)(128)(2,1)}, u32[]{:S(2)}, u32[]{:S(2)}) %collective-permute-start.12) | collective-permute-done | bytes 622624 | tf_op jit(solution)/shard_map/ppermute | solution.py:15
  389.2 1.9 constant_dynamic-update-slice_fusion.38
  394.4 1.9 constant_dynamic-update-slice_fusion.32
  396.4 2.9 dynamic-slice.3
  399.3 3.0 stack.172
  402.3 1.0 dynamic-slice.4
  403.9 3.0 pad_maximum_fusion
  407.0 1.0 copy.188
  (227 shorter events, 41.2 us)
Async XLA Ops:
  7.2 40.6 %copy-start = (bf16[128,256]{1,0:T(8,128)(2,1)S(1)}, bf16[128,256]{1,0:T(8,128)(2,1)}, u32[]{:S(2)}) copy-start(bf16[128,256]{1,0:T(8,128)(2,1)} %param.12) | copy-start | bytes 196612
  11.2 6.2 %copy-start.6 = (bf16[16,32,256]{2,1,0:T(8,128)(2,1)S(1)}, bf16[16,32,256]{2,1,0:T(8,128)(2,1)}, u32[]{:S(2)}) copy-start(bf16[16,32,256]{2,1,0:T(8,128)(2,1)} %param.15) | copy-start | bytes 786436
  11.2 9.5 %copy-start.25 = (bf16[256]{0:T(256)(128)(2,1)S(1)}, bf16[256]{0:T(256)(128)(2,1)}, u32[]{:S(2)}) copy-start(bf16[256]{0:T(256)(128)(2,1)} %param.13) | copy-start | bytes 1540
  11.2 32.4 %all-to-all-start = ((bf16[32,144,128]{2,1,0:T(8,128)(2,1)}), bf16[32,144,128]{2,1,0:T(8,128)(2,1)S(1)}, u32[]{:S(2)}, u32[]{:S(2)}) async-start(bf16[32,144,128]{2,1,0:T(8,128)(2,1)} %pad_maximum_fusion.5), calls=%async_computation | async-start | bytes 2359296 | tf_op jit(solution)/shard_map/all_to_all | solution.py:96
  17.4 284.9 %all-reduce.7.cloned.1.call-start = ((), (), s32[]{:S(2)}) async-start(), calls=%async_computation.2 | async-start | bytes 14417920
  17.5 10.9 %collective-permute-start.5 = (bf16[16,3,256]{2,1,0:T(4,128)(2,1)S(1)}, bf16[16,3,256]{2,1,0:T(4,128)(2,1)S(1)}, u32[]{:S(2)}, u32[]{:S(2)}) collective-permute-start(bf16[16,3,256]{2,1,0:T(4,128)(2,1)S(1)} %get-tuple-element.35), channel_id=1, source_target_pairs={{0,28},{4,0},{8,4},{12,8},{16,12},{20,16},{24,20},{28,24},{1,29},{... | collective-permute-start | bytes 73736 | tf_op jit(solution)/shard_map/ppermute | solution.py:37
  17.9 10.5 %collective-permute-start.4 = (bf16[16,3,256]{2,1,0:T(4,128)(2,1)S(1)}, bf16[16,3,256]{2,1,0:T(4,128)(2,1)S(1)}, u32[]{:S(2)}, u32[]{:S(2)}) collective-permute-start(bf16[16,3,256]{2,1,0:T(4,128)(2,1)S(1)} %get-tuple-element.34), channel_id=1, source_target_pairs={{0,4},{4,8},{8,12},{12,16},{16,20},{20,24},{24,28},{28,0},{1,5},{5... | collective-permute-start | bytes 73736 | tf_op jit(solution)/shard_map/ppermute | solution.py:36
  20.7 40.2 %copy-start.20 = (pred[22]{0:T(512)(128)(4,1)}, pred[22]{0:T(512)(128)(4,1)S(1)}, u32[]{:S(2)}) copy-start(pred[22]{0:T(512)(128)(4,1)S(1)} %compare_and_fusion.4) | copy-start | bytes 70
  47.7 11.8 %copy-start.14 = (bf16[512,128]{1,0:T(8,128)(2,1)}, bf16[512,128]{1,0:T(8,128)(2,1)S(1)}, u32[]{:S(2)}) copy-start(bf16[512,128]{1,0:T(8,128)(2,1)S(1)} %fusion.21) | copy-start | bytes 393220
  48.0 7.4 %collective-permute-start.1 = (bf16[16,6,256]{2,1,0:T(8,128)(2,1)S(1)}, bf16[16,6,256]{2,1,0:T(8,128)(2,1)S(1)}, u32[]{:S(2)}, u32[]{:S(2)}) collective-permute-start(bf16[16,6,256]{2,1,0:T(8,128)(2,1)S(1)} %get-tuple-element.37), channel_id=1, source_target_pairs={{0,28},{4,0},{8,4},{12,8},{16,12},{20,16},{24,20},{28,24},{1,29},{... | collective-permute-start | bytes 147464 | tf_op jit(solution)/shard_map/ppermute | solution.py:37
  49.6 5.9 %collective-permute-start = (bf16[16,6,256]{2,1,0:T(8,128)(2,1)S(1)}, bf16[16,6,256]{2,1,0:T(8,128)(2,1)S(1)}, u32[]{:S(2)}, u32[]{:S(2)}) collective-permute-start(bf16[16,6,256]{2,1,0:T(8,128)(2,1)S(1)} %get-tuple-element.36), channel_id=1, source_target_pairs={{0,4},{4,8},{8,12},{12,16},{16,20},{20,24},{24,28},{28,0},{1,5},{5... | collective-permute-start | bytes 147464 | tf_op jit(solution)/shard_map/ppermute | solution.py:36
  50.7 10.8 %collective-permute-start.7 = (bf16[3,38,256]{2,1,0:T(8,128)(2,1)S(1)}, bf16[3,38,256]{2,1,0:T(8,128)(2,1)S(1)}, u32[]{:S(2)}, u32[]{:S(2)}) collective-permute-start(bf16[3,38,256]{2,1,0:T(8,128)(2,1)S(1)} %get-tuple-element.27), channel_id=1, source_target_pairs={{1,0},{2,1},{3,2},{5,4},{6,5},{7,6},{9,8},{10,9},{11,10},{13,12},{... | collective-permute-start | bytes 175112 | tf_op jit(solution)/shard_map/ppermute | solution.py:40
  54.1 7.4 %collective-permute-start.6 = (bf16[3,38,256]{2,1,0:T(8,128)(2,1)S(1)}, bf16[3,38,256]{2,1,0:T(8,128)(2,1)S(1)}, u32[]{:S(2)}, u32[]{:S(2)}) collective-permute-start(bf16[3,38,256]{2,1,0:T(8,128)(2,1)S(1)} %get-tuple-element.26), channel_id=1, source_target_pairs={{0,1},{1,2},{2,3},{4,5},{5,6},{6,7},{8,9},{9,10},{10,11},{12,13},{... | collective-permute-start | bytes 175112 | tf_op jit(solution)/shard_map/ppermute | solution.py:39
  55.5 11.2 %copy-start.12 = (bf16[16,6,256]{2,1,0:T(8,128)(2,1)}, bf16[16,6,256]{2,1,0:T(8,128)(2,1)S(1)}, u32[]{:S(2)}) copy-start(bf16[16,6,256]{2,1,0:T(8,128)(2,1)S(1)} %collective-permute-done) | copy-start | bytes 147460
  55.6 6.9 %collective-permute-start.3 = (bf16[6,44,256]{2,1,0:T(8,128)(2,1)S(1)}, bf16[6,44,256]{2,1,0:T(8,128)(2,1)S(1)}, u32[]{:S(2)}, u32[]{:S(2)}) collective-permute-start(bf16[6,44,256]{2,1,0:T(8,128)(2,1)S(1)} %get-tuple-element.23), channel_id=1, source_target_pairs={{1,0},{2,1},{3,2},{5,4},{6,5},{7,6},{9,8},{10,9},{11,10},{13,12},{... | collective-permute-start | bytes 405512 | tf_op jit(solution)/shard_map/ppermute | solution.py:40
  59.6 6.9 %collective-permute-start.2 = (bf16[6,44,256]{2,1,0:T(8,128)(2,1)S(1)}, bf16[6,44,256]{2,1,0:T(8,128)(2,1)S(1)}, u32[]{:S(2)}, u32[]{:S(2)}) collective-permute-start(bf16[6,44,256]{2,1,0:T(8,128)(2,1)S(1)} %get-tuple-element.22), channel_id=1, source_target_pairs={{0,1},{1,2},{2,3},{4,5},{5,6},{6,7},{8,9},{9,10},{10,11},{12,13},{... | collective-permute-start | bytes 405512 | tf_op jit(solution)/shard_map/ppermute | solution.py:39
  61.5 5.4 %copy-start.16 = (bf16[3,38,256]{2,1,0:T(8,128)(2,1)}, bf16[3,38,256]{2,1,0:T(8,128)(2,1)S(1)}, u32[]{:S(2)}) copy-start(bf16[3,38,256]{2,1,0:T(8,128)(2,1)S(1)} %collective-permute-done.7) | copy-start | bytes 175108
  61.5 5.4 %copy-start.18 = (bf16[3,38,256]{2,1,0:T(8,128)(2,1)}, bf16[3,38,256]{2,1,0:T(8,128)(2,1)S(1)}, u32[]{:S(2)}) copy-start(bf16[3,38,256]{2,1,0:T(8,128)(2,1)S(1)} %collective-permute-done.6) | copy-start | bytes 175108
  66.5 0.7 copy-start.4
  67.1 0.7 copy-start.31
  71.4 1.1 copy-start.22
  74.0 1.7 copy-start.30
  79.3 2.0 copy-start.24
  80.0 1.3 copy-start.29
  83.4 1.0 copy-start.1
  83.4 1.0 copy-start.23
  88.8 1.0 copy-start.7
  88.8 1.0 copy-start.17
  88.8 1.0 copy-start.19
  88.8 1.0 copy-start.21
  90.1 0.7 copy-start.28
  96.5 0.7 copy-start.27
  98.6 0.9 copy-start.5
  98.6 0.9 copy-start.13
  107.8 0.7 copy-start.26
  109.7 0.9 copy-start.15
  117.7 39.6 %all-to-all-start.1 = ((bf16[32,128,128]{2,1,0:T(8,128)(2,1)}), bf16[32,128,128]{2,1,0:T(8,128)(2,1)S(1)}, u32[]{:S(2)}, u32[]{:S(2)}) async-start(bf16[32,128,128]{2,1,0:T(8,128)(2,1)} %bitcast.105), calls=%async_computation.1 | async-start | bytes 2097152 | tf_op jit(solution)/shard_map/all_to_all | solution.py:180
  303.2 7.0 %collective-permute-start.18 = (bf16[18432]{0:T(1024)(128)(2,1)S(1)}, bf16[18432]{0:T(1024)(128)(2,1)S(1)}, u32[]{:S(2)}, u32[]{:S(2)}) collective-permute-start(bf16[18432]{0:T(1024)(128)(2,1)S(1)} %get-tuple-element.13), channel_id=1, source_target_pairs={{0,31},{1,0},{2,1},{3,2},{4,3},{5,4},{6,5},{7,6},{8,7},{9,8},{10,9... | collective-permute-start | bytes 110600 | tf_op jit(solution)/shard_map/ppermute | solution.py:15
  305.1 7.0 %collective-permute-start.13 = (bf16[18432]{0:T(1024)(128)(2,1)S(1)}, bf16[18432]{0:T(1024)(128)(2,1)S(1)}, u32[]{:S(2)}, u32[]{:S(2)}) collective-permute-start(bf16[18432]{0:T(1024)(128)(2,1)S(1)} %get-tuple-element.11), channel_id=1, source_target_pairs={{0,31},{1,0},{2,1},{3,2},{4,3},{5,4},{6,5},{7,6},{8,7},{9,8},{10,9... | collective-permute-start | bytes 110600 | tf_op jit(solution)/shard_map/ppermute | solution.py:15
  306.9 7.1 %collective-permute-start.8 = (bf16[19456]{0:T(1024)(128)(2,1)S(1)}, bf16[19456]{0:T(1024)(128)(2,1)S(1)}, u32[]{:S(2)}, u32[]{:S(2)}) collective-permute-start(bf16[19456]{0:T(1024)(128)(2,1)S(1)} %get-tuple-element.9), channel_id=1, source_target_pairs={{0,31},{1,0},{2,1},{3,2},{4,3},{5,4},{6,5},{7,6},{8,7},{9,8},{10,9... | collective-permute-start | bytes 116744 | tf_op jit(solution)/shard_map/ppermute | solution.py:15
  310.2 11.9 %collective-permute-start.19 = (bf16[36864]{0:T(1024)(128)(2,1)S(1)}, bf16[36864]{0:T(1024)(128)(2,1)S(1)}, u32[]{:S(2)}, u32[]{:S(2)}) collective-permute-start(bf16[36864]{0:T(1024)(128)(2,1)S(1)} %pad_maximum_fusion.25), channel_id=1, source_target_pairs={{0,30},{1,31},{2,0},{3,1},{4,2},{5,3},{6,4},{7,5},{8,6},{9,7},{10,... | collective-permute-start | bytes 221192 | tf_op jit(solution)/shard_map/ppermute | solution.py:15
  312.1 11.6 %collective-permute-start.14 = (bf16[36864]{0:T(1024)(128)(2,1)S(1)}, bf16[36864]{0:T(1024)(128)(2,1)S(1)}, u32[]{:S(2)}, u32[]{:S(2)}) collective-permute-start(bf16[36864]{0:T(1024)(128)(2,1)S(1)} %pad_maximum_fusion.24), channel_id=1, source_target_pairs={{0,30},{1,31},{2,0},{3,1},{4,2},{5,3},{6,4},{7,5},{8,6},{9,7},{10,... | collective-permute-start | bytes 221192 | tf_op jit(solution)/shard_map/ppermute | solution.py:15
  314.1 10.6 %collective-permute-start.9 = (bf16[38912]{0:T(1024)(128)(2,1)S(1)}, bf16[38912]{0:T(1024)(128)(2,1)S(1)}, u32[]{:S(2)}, u32[]{:S(2)}) collective-permute-start(bf16[38912]{0:T(1024)(128)(2,1)S(1)} %pad_maximum_fusion.23), channel_id=1, source_target_pairs={{0,30},{1,31},{2,0},{3,1},{4,2},{5,3},{6,4},{7,5},{8,6},{9,7},{10,... | collective-permute-start | bytes 233480 | tf_op jit(solution)/shard_map/ppermute | solution.py:15
  322.1 5.5 %collective-permute-start.20 = (bf16[73728]{0:T(1024)(128)(2,1)S(1)}, bf16[73728]{0:T(1024)(128)(2,1)S(1)}, u32[]{:S(2)}, u32[]{:S(2)}) collective-permute-start(bf16[73728]{0:T(1024)(128)(2,1)S(1)} %pad_maximum_fusion.22), channel_id=1, source_target_pairs={{0,28},{1,29},{2,30},{3,31},{4,0},{5,1},{6,2},{7,3},{8,4},{9,5},{1... | collective-permute-start | bytes 442376 | tf_op jit(solution)/shard_map/ppermute | solution.py:15
  323.7 5.5 %collective-permute-start.15 = (bf16[73728]{0:T(1024)(128)(2,1)S(1)}, bf16[73728]{0:T(1024)(128)(2,1)S(1)}, u32[]{:S(2)}, u32[]{:S(2)}) collective-permute-start(bf16[73728]{0:T(1024)(128)(2,1)S(1)} %pad_maximum_fusion.21), channel_id=1, source_target_pairs={{0,28},{1,29},{2,30},{3,31},{4,0},{5,1},{6,2},{7,3},{8,4},{9,5},{1... | collective-permute-start | bytes 442376 | tf_op jit(solution)/shard_map/ppermute | solution.py:15
  324.7 6.2 %copy-start.10 = (bf16[38912]{0:T(1024)(128)(2,1)}, bf16[38912]{0:T(1024)(128)(2,1)S(1)}, u32[]{:S(2)}) copy-start(bf16[38912]{0:T(1024)(128)(2,1)S(1)} %collective-permute-done.9) | copy-start | bytes 233476
  324.7 6.2 %collective-permute-start.10 = (bf16[77824]{0:T(1024)(128)(2,1)S(1)}, bf16[77824]{0:T(1024)(128)(2,1)S(1)}, u32[]{:S(2)}, u32[]{:S(2)}) collective-permute-start(bf16[77824]{0:T(1024)(128)(2,1)S(1)} %pad_maximum_fusion.17), channel_id=1, source_target_pairs={{0,28},{1,29},{2,30},{3,31},{4,0},{5,1},{6,2},{7,3},{8,4},{9,5},{1... | collective-permute-start | bytes 466952 | tf_op jit(solution)/shard_map/ppermute | solution.py:15
  327.7 10.0 %collective-permute-start.21 = (bf16[147456]{0:T(1024)(128)(2,1)S(1)}, bf16[147456]{0:T(1024)(128)(2,1)S(1)}, u32[]{:S(2)}, u32[]{:S(2)}) collective-permute-start(bf16[147456]{0:T(1024)(128)(2,1)S(1)} %pad_maximum_fusion.12), channel_id=1, source_target_pairs={{0,24},{1,25},{2,26},{3,27},{4,28},{5,29},{6,30},{7,31},{8,0},{9,1... | collective-permute-start | bytes 884744 | tf_op jit(solution)/shard_map/ppermute | solution.py:15
  329.3 14.8 %collective-permute-start.16 = (bf16[147456]{0:T(1024)(128)(2,1)S(1)}, bf16[147456]{0:T(1024)(128)(2,1)S(1)}, u32[]{:S(2)}, u32[]{:S(2)}) collective-permute-start(bf16[147456]{0:T(1024)(128)(2,1)S(1)} %pad_maximum_fusion.11), channel_id=1, source_target_pairs={{0,24},{1,25},{2,26},{3,27},{4,28},{5,29},{6,30},{7,31},{8,0},{9,1... | collective-permute-start | bytes 884744 | tf_op jit(solution)/shard_map/ppermute | solution.py:15
  330.9 13.2 %copy-start.2 = (bf16[77824]{0:T(1024)(128)(2,1)}, bf16[77824]{0:T(1024)(128)(2,1)S(1)}, u32[]{:S(2)}) copy-start(bf16[77824]{0:T(1024)(128)(2,1)S(1)} %collective-permute-done.10) | copy-start | bytes 466948
  330.9 19.4 %collective-permute-start.11 = (bf16[155648]{0:T(1024)(128)(2,1)S(1)}, bf16[155648]{0:T(1024)(128)(2,1)S(1)}, u32[]{:S(2)}, u32[]{:S(2)}) collective-permute-start(bf16[155648]{0:T(1024)(128)(2,1)S(1)} %pad_maximum_fusion.10), channel_id=1, source_target_pairs={{0,24},{1,25},{2,26},{3,27},{4,28},{5,29},{6,30},{7,31},{8,0},{9,1... | collective-permute-start | bytes 933896 | tf_op jit(solution)/shard_map/ppermute | solution.py:15
  337.8 25.3 %collective-permute-start.22 = (bf16[294912]{0:T(1024)(128)(2,1)S(1)}, bf16[294912]{0:T(1024)(128)(2,1)S(1)}, u32[]{:S(2)}, u32[]{:S(2)}) collective-permute-start(bf16[294912]{0:T(1024)(128)(2,1)S(1)} %get-tuple-element.32), channel_id=1, source_target_pairs={{0,16},{1,17},{2,18},{3,19},{4,20},{5,21},{6,22},{7,23},{8,24},{9,... | collective-permute-start | bytes 1769480 | tf_op jit(solution)/shard_map/ppermute | solution.py:15
  344.1 31.6 %collective-permute-start.17 = (bf16[294912]{0:T(1024)(128)(2,1)S(1)}, bf16[294912]{0:T(1024)(128)(2,1)S(1)}, u32[]{:S(2)}, u32[]{:S(2)}) collective-permute-start(bf16[294912]{0:T(1024)(128)(2,1)S(1)} %get-tuple-element.30), channel_id=1, source_target_pairs={{0,16},{1,17},{2,18},{3,19},{4,20},{5,21},{6,22},{7,23},{8,24},{9,... | collective-permute-start | bytes 1769480 | tf_op jit(solution)/shard_map/ppermute | solution.py:15
  350.3 17.3 %copy-start.8 = (bf16[155648]{0:T(1024)(128)(2,1)}, bf16[155648]{0:T(1024)(128)(2,1)S(1)}, u32[]{:S(2)}) copy-start(bf16[155648]{0:T(1024)(128)(2,1)S(1)} %collective-permute-done.11) | copy-start | bytes 933892
  351.3 37.9 %collective-permute-start.12 = (bf16[311296]{0:T(1024)(128)(2,1)}, bf16[311296]{0:T(1024)(128)(2,1)}, u32[]{:S(2)}, u32[]{:S(2)}) collective-permute-start(bf16[311296]{0:T(1024)(128)(2,1)} %get-tuple-element.28), channel_id=1, source_target_pairs={{0,16},{1,17},{2,18},{3,19},{4,20},{5,21},{6,22},{7,23},{8,24},{9,... | collective-permute-start | bytes 1867784 | tf_op jit(solution)/shard_map/ppermute | solution.py:15
  383.9 8.5 %copy-start.11 = (bf16[38912]{0:T(1024)(128)(2,1)S(1)}, bf16[38912]{0:T(1024)(128)(2,1)}, u32[]{:S(2)}) copy-start(bf16[38912]{0:T(1024)(128)(2,1)} %copy-done.10) | copy-start | bytes 233476
  383.9 9.1 %copy-start.3 = (bf16[77824]{0:T(1024)(128)(2,1)S(1)}, bf16[77824]{0:T(1024)(128)(2,1)}, u32[]{:S(2)}) copy-start(bf16[77824]{0:T(1024)(128)(2,1)} %copy-done.2) | copy-start | bytes 466948
  383.9 9.8 %copy-start.9 = (bf16[155648]{0:T(1024)(128)(2,1)S(1)}, bf16[155648]{0:T(1024)(128)(2,1)}, u32[]{:S(2)}) copy-start(bf16[155648]{0:T(1024)(128)(2,1)} %copy-done.8) | copy-start | bytes 933892
Sparse Core Ops, SparseCore 0:
  115.1 187.1 all-reduce.6
